TPU v7x, 256 devices: a whole 4x4x8 slice. The times are simulated.
256 devices in a mesh: mem: 8 (over x, y_hi), lat: 32 (over y_lo, z, core).
Axes of the slice: x: 4, y: 4 (y_hi: 2, y_lo: 2; y = y_hi * 2 + y_lo), z: 8, core: 2. Of those that a mesh axis runs over, the one named last changes fastest.
Arguments:
- cotangent: bfloat16 [8, 3, 4, 1024, 4096], P('mem', None, None, 'lat'), may hold values from -6 to 6
- legendre: bfloat16 [704, 2, 352, 512], P('lat', None, None, 'mem'), may hold values from -0.25 to 0.25
- wave_order: int32 [704], replicated, may hold values from 0 to 703, each once
- mode_depth: float32 [4], replicated, may hold values from 0.5 to 20
- diffusion: float32 [4], replicated, may hold values from 0.5 to 8
- quad_weights: float32 [512], replicated, may hold values from 0.25 to 2.5
Outputs:
- adjoint: bfloat16 [8, 3, 4, 1024, 4096], P('mem', None, None, 'lat')
Inputs may be any that keep to these rules, and one draw needn't show every extreme that they name: `wave_order`: each zonal wavenumber 0 to 703 appears exactly once; legendre's first index follows this order.
All inputs are finite; a program needn't handle non-finite values.
Results may differ from a plain program's by a relative error of at most 0.0076.
Values may be sent and summed in bfloat16 or wider, within the bound.
No kernel may reach another device: no remote copies, remote signals or barrier semaphores. Data moves between devices by JAX's collectives and lax.ppermute only.
A program may use at most 192 MiB of HBM per device.

v0:
```python
import math

import jax
import jax.numpy as jnp
from jax import lax
from jax.sharding import PartitionSpec as P


def fourier_table(waves, valid, lon_count):
    inner = 1 << (lon_count.bit_length() - 1) // 2
    outer = lon_count // inner
    step = jnp.float32(2.0 * math.pi / lon_count)
    even = (jnp.arange(waves.size, dtype=jnp.int32) % 2 == 0)[None, :]
    waves = waves.reshape(1, -1)
    valid = valid.reshape(1, -1)
    phase_a = (jnp.arange(outer, dtype=jnp.int32)[:, None] * inner * waves) % lon_count
    phase_b = (jnp.arange(inner, dtype=jnp.int32)[:, None] * waves) % lon_count
    angle_a = phase_a.astype(jnp.float32) * step
    angle_b = phase_b.astype(jnp.float32) * step
    cos_a, sin_a = jnp.cos(angle_a), jnp.sin(angle_a)
    cos_b, sin_b = jnp.cos(angle_b), jnp.sin(angle_b)
    zero = jnp.zeros_like(cos_a)
    u = jnp.where(valid, jnp.where(even, cos_a, -sin_a), zero)
    v = jnp.where(valid, jnp.where(even, -sin_a, -cos_a), zero)
    table = u[:, None, :] * cos_b[None, :, :] + v[:, None, :] * sin_b[None, :, :]
    table = table.reshape(lon_count, -1).astype(jnp.bfloat16)
    return lax.optimization_barrier(table)


def implicit(values, degree, top_degree, mode_depth, diffusion):
    shape = values.shape
    levels = mode_depth.shape[0]
    values = values.reshape(shape[:-1] + (3, levels))
    degree_f = degree.astype(jnp.float32)
    scaled = (degree_f * (degree_f + 1.0) / (top_degree * (top_degree + 1.0)))[
        :, :, :, None, None, None
    ]
    vorticity = values[..., 0, :] / (1.0 + diffusion * scaled * scaled)
    damping = 1.0 / (1.0 + mode_depth * scaled)
    divergence = damping * (values[..., 1, :] - mode_depth * values[..., 2, :])
    height = damping * (scaled * values[..., 1, :] + values[..., 2, :])
    joined = jnp.stack([vorticity, divergence, height], axis=-2)
    return joined.reshape(shape).astype(jnp.bfloat16)


def shards(cotangent, legendre, wave_order, mode_depth, diffusion, quad_weights):
    members, fields, levels, band_rows, lon_count = cotangent.shape
    lat_count = lax.axis_size("lat")
    mem_count = lax.axis_size("mem")
    half_count = lat_count // 2
    total_waves = wave_order.shape[0]
    count_waves = total_waves // lat_count
    group = -(-count_waves // mem_count)
    padded = group * mem_count
    half_deg = legendre.shape[2]
    slab = legendre.shape[3]
    half_lat = slab * mem_count
    channels = fields * levels
    width = channels * band_rows
    top_degree = float(total_waves + 2 * half_deg - 2)
    lat_id = lax.axis_index("lat")
    mem_id = lax.axis_index("mem")

    basis = jnp.pad(legendre, ((0, padded - count_waves), (0, 0), (0, 0), (0, 0)))
    basis = basis.reshape(mem_count, group, 2, half_deg, slab)
    basis = lax.all_to_all(basis, "mem", 0, 0, tiled=True)
    basis = jnp.transpose(basis, (1, 2, 3, 0, 4)).reshape(group, 2, half_deg, half_lat)

    slot = jnp.arange(padded, dtype=jnp.int32)
    index = jnp.arange(lat_count, dtype=jnp.int32)[:, None] * count_waves + slot[None, :]
    index = jnp.minimum(index, total_waves - 1)
    column_waves = jnp.repeat(jnp.take(wave_order, index), 2, axis=1)
    valid = jnp.broadcast_to((slot < count_waves)[None, :], (lat_count, padded))
    valid = jnp.repeat(valid, 2, axis=1)
    table = fourier_table(column_waves, valid, lon_count)
    flattened = cotangent.reshape(width, lon_count)
    factor = jnp.where(column_waves == 0, 1.0, 2.0).astype(jnp.float32).reshape(-1)
    coeffs = lax.dot_general(
        table, flattened, (((0,), (1,)), ((), ())), preferred_element_type=jnp.float32
    )
    coeffs = (coeffs * factor[:, None]).astype(jnp.bfloat16)
    coeffs = coeffs.reshape(lat_count, padded * 2, width)
    received = lax.all_to_all(coeffs, "lat", 0, 0, tiled=True)
    received = received.reshape(lat_count, mem_count, group, 2, channels, band_rows)
    northern = received[:half_count].astype(jnp.float32)
    southern = received[half_count:].astype(jnp.float32)
    even_part = (northern + southern).astype(jnp.bfloat16)
    odd_part = (northern - southern).astype(jnp.bfloat16)
    parts = jnp.stack([even_part, odd_part], axis=0)
    parts = jnp.transpose(parts, (2, 3, 0, 4, 5, 1, 6)).reshape(
        mem_count, group * 2 * 2 * channels, half_lat
    )
    parts = lax.all_to_all(parts, "mem", 0, 0, tiled=True)
    parts = parts.reshape(mem_count, group, 2, 2, channels, half_lat)

    analysed = jnp.einsum(
        "kpiy,ekpqcy->kpieqc", basis, parts, preferred_element_type=jnp.float32
    )
    local = mem_id * group + jnp.arange(group, dtype=jnp.int32)
    index = jnp.minimum(lat_id * count_waves + local, total_waves - 1)
    own_waves = jnp.take(wave_order, index)
    degree = (
        own_waves[:, None, None]
        + 2 * jnp.arange(half_deg, dtype=jnp.int32)[None, None, :]
        + jnp.arange(2, dtype=jnp.int32)[None, :, None]
    )
    spectral = implicit(analysed, degree, top_degree, mode_depth, diffusion)
    synth = jnp.einsum(
        "kpieqc,kpiy->pekqcy", spectral, basis, preferred_element_type=jnp.float32
    )
    gridded = jnp.stack(
        [quad_weights * (synth[0] + synth[1]), quad_weights * (synth[0] - synth[1])], axis=4
    ).astype(jnp.bfloat16)
    gridded = gridded.reshape(mem_count, group * 2 * channels, 2 * half_lat)
    gridded = lax.all_to_all(gridded, "mem", 0, 0, tiled=True)
    gridded = gridded.reshape(mem_count, group, 2, channels, lat_count, band_rows)
    gridded = jnp.transpose(gridded, (4, 0, 1, 2, 3, 5)).reshape(lat_count, padded * 2, width)
    returned = lax.all_to_all(gridded, "lat", 0, 0, tiled=True)
    returned = returned.reshape(lat_count * padded * 2, width)

    result = lax.dot_general(
        returned, table, (((0,), (1,)), ((), ())), preferred_element_type=jnp.float32
    )
    result = result * jnp.float32(1.0 / lon_count)
    return result.astype(jnp.bfloat16).reshape(members, fields, levels, band_rows, lon_count)


def solution(mesh):
    placed = (P("mem", None, None, "lat", None), P("lat", None, None, "mem"), P(), P(), P(), P())
    return jax.shard_map(
        shards,
        mesh=mesh,
        in_specs=placed,
        out_specs=P("mem", None, None, "lat", None),
        check_vma=False,
    )
```

profile of v0, /device:TPU:32, one launch (start us, length us, event | category | flops | bytes accessed | tf_op | source)
XLA Modules:
  0.0 238.7 jit_solution(12540071874744602399)
XLA Ops:
  1.3 3.2 %gather_fusion = s32[768]{0:T(1024)S(1)} fusion(s32[704]{0:T(1024)S(1)} %copy-done.2, s32[1024]{0:T(1024)S(1)} %pad_clamp_fusion.1), kind=kCustom, calls=%fused_computation | custom fusion | bytes 9216 | tf_op jit(solution)/shard_map/jit(_take)/gather | solution.py:72
  5.5 0.6 compare_select_fusion.2
  6.1 4.7 %select_select_fusion.1 = (f32[64,1536]{1,0:T(8,128)S(1)}, f32[64,1536]{1,0:T(8,128)}, f32[64,1536]{1,0:T(8,128)}, f32[64,1536]{1,0:T(8,128)}) fusion(s32[1536]{0:T(1024)S(1)} %mul.263, s32[64]{0:T(128)} %iota_multiply_fusion.2, pred[1536]{0:T(1024)(128)(4,1)} %fusion.29, pred[1536]{0:T(1024)(128)(4,1)S(1)} %broadcast_in_dim.68), kind=kLoop, calls=%fused_computation.43 | loop fusion | flops 3342336 | bytes 1582336 | tf_op jit(solution)/shard_map/jit(_where)/select_n | solution.py:23
  10.7 10.4 %add_convert_fusion = bf16[64,64,1536]{2,1,0:T(8,128)(2,1)} fusion(f32[64,1536]{1,0:T(8,128)} %get-tuple-element.16, f32[64,1536]{1,0:T(8,128)} %get-tuple-element.13, f32[64,1536]{1,0:T(8,128)} %get-tuple-element.17, f32[64,1536]{1,0:T(8,128)S(1)} %get-tuple-element.12), kind=kLoop, calls=%fused_computation.2 | loop fusion | flops 25165824 | bytes 14155776 | tf_op jit(solution)/shard_map/convert_element_type | solution.py:26
  21.1 10.8 %fusion = bf16[1536,384]{1,0:T(8,128)(2,1)} fusion(bf16[4096,1536]{1,0:T(8,128)(2,1)} %bitcast.45, bf16[384,4096]{1,0:T(8,128)(2,1)S(1)} %bitcast.43, f32[1536]{0:T(1024)S(1)} %copy-done.5), kind=kOutput, calls=%fused_computation.7 | convolution fusion | flops 4833017856 | bytes 16914432 | tf_op jit(solution)/shard_map/dot_general | solution.py:78
  31.9 9.7 %all-to-all-start.1 = ((bf16[32,48,384]{2,1,0:T(8,128)(2,1)}), bf16[32,48,384]{2,1,0:T(8,128)(2,1)S(1)}, u32[]{:S(2)}, u32[]{:S(2)}) async-start(bf16[32,48,384]{2,1,0:T(8,128)(2,1)} %bitcast.51), calls=%async_computation.1 | async-start | bytes 2359296 | tf_op jit(solution)/shard_map/all_to_all | solution.py:83
  41.6 3.5 %pad.4 = bf16[24,2,352,64]{2,3,1,0:T(8,128)(2,1)} pad(bf16[22,2,352,64]{2,3,1,0:T(8,128)(2,1)} %param.7, bf16[]{:T(256)} %constant.51.clone.1), padding=0_2x0_0x0_0x0_0 | pad | bytes 4145154 | tf_op jit(solution)/shard_map/jit(_pad)/pad | solution.py:64
  45.1 28.3 %all-to-all-done.1 = bf16[32,48,384]{2,1,0:T(8,128)(2,1)S(1)} async-done(((bf16[32,48,384]{2,1,0:T(8,128)(2,1)}), bf16[32,48,384]{2,1,0:T(8,128)(2,1)S(1)}, u32[]{:S(2)}, u32[]{:S(2)}) %all-to-all-start.1) | async-done | bytes 1179680 | tf_op jit(solution)/shard_map/all_to_all | solution.py:83
  73.4 6.6 %all-to-all-start = ((bf16[8,3,2,352,64]{3,4,2,1,0:T(8,128)(2,1)}), bf16[8,3,2,352,64]{3,4,2,1,0:T(8,128)(2,1)}, u32[]{:S(2)}, u32[]{:S(2)}) async-start(bf16[8,3,2,352,64]{3,4,2,1,0:T(8,128)(2,1)} %bitcast), calls=%async_computation | async-start | bytes 4718592 | tf_op jit(solution)/shard_map/all_to_all | solution.py:66
  80.1 1.3 fusion.8
  81.4 3.6 %convert_element_type.112 = bf16[1,16,8,3,2,12,32]{6,5,4,3,2,1,0:T(8,128)(2,1)S(1)} reshape(bf16[16,48,384]{2,1,0:T(8,128)(2,1)} %get-tuple-element.10) | data formatting | bytes 1179648 | tf_op jit(solution)/shard_map/convert_element_type | solution.py:87
  85.0 4.7 %convert_element_type.114 = bf16[1,16,8,3,2,12,32]{6,5,4,3,2,1,0:T(8,128)(2,1)} reshape(bf16[16,48,384]{2,1,0:T(8,128)(2,1)} %get-tuple-element.11) | data formatting | bytes 1179648 | tf_op jit(solution)/shard_map/convert_element_type | solution.py:88
  89.7 3.5 %maximum_bitcast_fusion = bf16[8,3,2,2,12,16,32]{6,4,3,1,0,5,2:T(8,128)(2,1)S(1)} fusion(bf16[1,16,8,3,2,12,32]{6,5,4,3,2,1,0:T(8,128)(2,1)} %convert_element_type.114, bf16[1,16,8,3,2,12,32]{6,5,4,3,2,1,0:T(8,128)(2,1)S(1)} %convert_element_type.112), kind=kLoop, calls=%fused_computation.3 | loop fusion | flops 589824 | bytes 2359296 | tf_op jit(solution)/shard_map/transpose | solution.py:90
  93.2 7.5 %copy.21 = bf16[8,3,2,2,12,16,32]{6,5,4,3,2,1,0:T(8,128)(2,1)} copy(bf16[8,3,2,2,12,16,32]{6,4,3,1,0,5,2:T(8,128)(2,1)S(1)} %maximum_bitcast_fusion) | data formatting | bytes 2359296 | tf_op jit(solution)/shard_map/transpose | solution.py:90
  100.8 7.3 %reshape.508 = bf16[8,144,512]{2,1,0:T(8,128)(2,1)} reshape(bf16[8,3,2,2,12,16,32]{6,5,4,3,2,1,0:T(8,128)(2,1)} %copy.21) | data formatting | bytes 2359296 | tf_op jit(solution)/shard_map/reshape | solution.py:90
  108.1 6.2 %all-to-all-done = bf16[8,3,2,352,64]{3,4,2,1,0:T(8,128)(2,1)} async-done(((bf16[8,3,2,352,64]{3,4,2,1,0:T(8,128)(2,1)}), bf16[8,3,2,352,64]{3,4,2,1,0:T(8,128)(2,1)}, u32[]{:S(2)}, u32[]{:S(2)}) %all-to-all-start) | async-done | bytes 2162720 | tf_op jit(solution)/shard_map/all_to_all | solution.py:66
  114.3 4.5 %all-to-all-start.2 = ((bf16[8,144,512]{2,1,0:T(8,128)(2,1)}), bf16[8,144,512]{2,1,0:T(8,128)(2,1)}, u32[]{:S(2)}, u32[]{:S(2)}) async-start(bf16[8,144,512]{2,1,0:T(8,128)(2,1)} %reshape.508), calls=%async_computation.2 | async-start | bytes 2359296 | tf_op jit(solution)/shard_map/all_to_all | solution.py:93
  118.8 0.6 gather_fusion.1
  119.7 1.9 copy.20
  121.6 13.3 %all-to-all-done.2 = bf16[8,144,512]{2,1,0:T(8,128)(2,1)} async-done(((bf16[8,144,512]{2,1,0:T(8,128)(2,1)}), bf16[8,144,512]{2,1,0:T(8,128)(2,1)}, u32[]{:S(2)}, u32[]{:S(2)}) %all-to-all-start.2) | async-done | bytes 1179680 | tf_op jit(solution)/shard_map/all_to_all | solution.py:93
  134.9 1.9 copy.22
  136.8 0.8 fusion.34
  138.2 1.1 copy-done.4
  139.3 1.0 fusion.3
  141.0 1.2 copy.28
  142.2 0.9 convert_element_type.117
  143.1 21.9 %all_to_all.25 = bf16[8,72,1024]{2,1,0:T(8,128)(2,1)S(1)} all-to-all(bf16[8,72,1024]{2,1,0:T(8,128)(2,1)S(1)} %convert_element_type.117), channel_id=1, replica_groups=mesh['mem'=8,'lat'=32] {'mem'}, dimensions={0} | all-to-all | bytes 2359296 | tf_op jit(solution)/shard_map/all_to_all | solution.py:115
  165.0 4.7 %reshape.511 = bf16[8,3,2,12,32,32]{5,4,3,2,1,0:T(8,128)(2,1)} reshape(bf16[8,72,1024]{2,1,0:T(8,128)(2,1)S(1)} %all_to_all.25) | data formatting | bytes 2359296 | tf_op jit(solution)/shard_map/reshape | solution.py:116
  169.8 7.0 %copy.45 = bf16[8,3,2,12,32,32]{5,3,2,1,0,4:T(8,128)(2,1)} copy(bf16[8,3,2,12,32,32]{5,4,3,2,1,0:T(8,128)(2,1)} %reshape.511) | data formatting | bytes 2359296 | tf_op jit(solution)/shard_map/reshape | solution.py:116
  176.7 7.4 %reshape.512 = bf16[32,48,384]{2,1,0:T(8,128)(2,1)S(1)} reshape(bf16[32,8,3,2,12,32]{5,4,3,2,1,0:T(8,128)(2,1)} %bitcast.44) | data formatting | bytes 2359296 | tf_op jit(solution)/shard_map/reshape | solution.py:117
  184.1 36.0 %all_to_all.26 = bf16[32,48,384]{2,1,0:T(8,128)(2,1)S(1)} all-to-all(bf16[32,48,384]{2,1,0:T(8,128)(2,1)S(1)} %reshape.512), channel_id=1, replica_groups=mesh['mem'=8,'lat'=32] {'lat'}, dimensions={0} | all-to-all | bytes 2359296 | tf_op jit(solution)/shard_map/all_to_all | solution.py:118
  220.1 18.6 %multiply_convert_fusion = bf16[384,4096]{1,0:T(8,128)(2,1)} fusion(bf16[1536,384]{1,0:T(8,128)(2,1)S(1)} %bitcast.52, bf16[4096,1536]{1,0:T(8,128)(2,1)} %bitcast.46), kind=kOutput, calls=%fused_computation.5 | convolution fusion | flops 4834983936 | bytes 16908288 | tf_op jit(solution)/shard_map/dot_general | solution.py:121
  (41 shorter events, 3.6 us)
Async XLA Ops:
  0.0 21.1 %copy-start = (bf16[1,3,4,32,4096]{4,3,2,1,0:T(8,128)(2,1)S(1)}, bf16[1,3,4,32,4096]{4,3,2,1,0:T(8,128)(2,1)}, u32[]{:S(2)}) copy-start(bf16[1,3,4,32,4096]{4,3,2,1,0:T(8,128)(2,1)} %param.6) | copy-start | bytes 9437188
  0.0 1.3 copy-start.2
  10.7 10.4 %copy-start.5 = (f32[1536]{0:T(1024)S(1)}, f32[1536]{0:T(1024)}, u32[]{:S(2)}) copy-start(f32[1536]{0:T(1024)} %compare_select_fusion.2) | copy-start | bytes 18436
  31.9 41.5 %all-to-all-start.1 = ((bf16[32,48,384]{2,1,0:T(8,128)(2,1)}), bf16[32,48,384]{2,1,0:T(8,128)(2,1)S(1)}, u32[]{:S(2)}, u32[]{:S(2)}) async-start(bf16[32,48,384]{2,1,0:T(8,128)(2,1)} %bitcast.51), calls=%async_computation.1 | async-start | bytes 2359296 | tf_op jit(solution)/shard_map/all_to_all | solution.py:83
  73.4 40.9 %all-to-all-start = ((bf16[8,3,2,352,64]{3,4,2,1,0:T(8,128)(2,1)}), bf16[8,3,2,352,64]{3,4,2,1,0:T(8,128)(2,1)}, u32[]{:S(2)}, u32[]{:S(2)}) async-start(bf16[8,3,2,352,64]{3,4,2,1,0:T(8,128)(2,1)} %bitcast), calls=%async_computation | async-start | bytes 4718592 | tf_op jit(solution)/shard_map/all_to_all | solution.py:66
  108.1 11.5 %copy-start.7 = (f32[4]{0:T(128)S(1)}, f32[4]{0:T(128)}, u32[]{:S(2)}) copy-start(f32[4]{0:T(128)} %param.9) | copy-start | bytes 52
  108.1 11.5 %copy-start.8 = (f32[4]{0:T(128)S(1)}, f32[4]{0:T(128)}, u32[]{:S(2)}) copy-start(f32[4]{0:T(128)} %param.10) | copy-start | bytes 52
  114.3 20.6 %all-to-all-start.2 = ((bf16[8,144,512]{2,1,0:T(8,128)(2,1)}), bf16[8,144,512]{2,1,0:T(8,128)(2,1)}, u32[]{:S(2)}, u32[]{:S(2)}) async-start(bf16[8,144,512]{2,1,0:T(8,128)(2,1)} %reshape.508), calls=%async_computation.2 | async-start | bytes 2359296 | tf_op jit(solution)/shard_map/all_to_all | solution.py:93
  121.6 16.0 %copy-start.3 = (bf16[3,2,352,8,64]{2,4,3,1,0:T(8,128)(2,1)}, bf16[3,2,352,8,64]{2,4,3,1,0:T(8,128)(2,1)S(1)}, u32[]{:S(2)}) copy-start(bf16[3,2,352,8,64]{2,4,3,1,0:T(8,128)(2,1)S(1)} %copy.20) | copy-start | bytes 6488068
  137.6 1.7 copy-start.4
  139.3 1.0 copy-start.6
  220.1 18.6 %copy-start.1 = (bf16[1,3,4,32,4096]{4,3,2,1,0:T(8,128)(2,1)S(1)}, bf16[1,3,4,32,4096]{4,3,2,1,0:T(8,128)(2,1)}, u32[]{:S(2)}) copy-start(bf16[1,3,4,32,4096]{4,3,2,1,0:T(8,128)(2,1)} %param.6) | copy-start | bytes 9437188
where the time goes:
time: 241 us; the launch traced here: 239 us
  blocking collectives  57.9 us (24%)
  local copies, waits for them, and re-layouts  57.5 us (24%)
  waiting for transfers between devices  47.8 us (20%)
  matrix products  31.2 us (13%)
  other arithmetic  23.1 us (10%)
  starting transfers between devices  20.9 us (9%)
    all_to_all x1, blocking collectives, shards(): returned = lax.all_to_all(gridded, 'lat', 0, 0, tiled=True)  36 us
    all_to_all x1, waiting for transfers between devices, shards(): received = lax.all_to_all(coeffs, 'lat', 0, 0, tiled=True)  28.3 us
    all_to_all x1, blocking collectives, shards(): gridded = lax.all_to_all(gridded, 'mem', 0, 0, tiled=True)  21.9 us
    dot_general x1, matrix products, shards(): lax.dot_general(returned, table, (((0,), (1,)), ((), ())), preferred_elem...  18.6 us
    all_to_all x1, waiting for transfers between devices, shards(): parts = lax.all_to_all(parts, 'mem', 0, 0, tiled=True)  13.3 us
    reshape x2, local copies, waits for them, and re-layouts, shards(): gridded.reshape(mem_count, group, 2, channels, lat_count, band_rows)  11.7 us
    dot_general x1, matrix products, shards(): lax.dot_general(table, flattened, (((0,), (1,)), ((), ())), preferred_ele...  10.8 us
    convert_element_type x1, other arithmetic, fourier_table(): table = table.reshape(lon_count, -1).astype(jnp.bfloat16)  10.4 us
  transfers between devices with their start and end apart: 3, of which 3 were waited for; matrix products, arithmetic and copies ran while one was open for 14% of the time, Pallas kernels for 0%

commit v1 on v0

--- a/solution.py
+++ b/solution.py
@@ -81,12 +81,12 @@
     coeffs = (coeffs * factor[:, None]).astype(jnp.bfloat16)
     coeffs = coeffs.reshape(lat_count, padded * 2, width)
     received = lax.all_to_all(coeffs, "lat", 0, 0, tiled=True)
-    received = received.reshape(lat_count, mem_count, group, 2, channels, band_rows)
     northern = received[:half_count].astype(jnp.float32)
     southern = received[half_count:].astype(jnp.float32)
     even_part = (northern + southern).astype(jnp.bfloat16)
     odd_part = (northern - southern).astype(jnp.bfloat16)
     parts = jnp.stack([even_part, odd_part], axis=0)
+    parts = parts.reshape(2, half_count, mem_count, group, 2, channels, band_rows)
     parts = jnp.transpose(parts, (2, 3, 0, 4, 5, 1, 6)).reshape(
         mem_count, group * 2 * 2 * channels, half_lat
     )

time: 241 us -> 241 us (level)
    another operation x0 -> x2, local copies, waits for them, and re-layouts: none -> 8.32 us  [shards(): parts = jnp.stack([even_part, odd_part], axis=0)]
    convert_element_type x2 -> x0, local copies, waits for them, and re-layouts: 8.32 us -> none  [the longest x1 4.69 us: shards(): odd_part = (northern - southern).astype(jnp.bfloat16)]
where the time goes in v1:
time: 241 us; the launch traced here: 239 us
  blocking collectives  57.9 us (24%)
  local copies, waits for them, and re-layouts  57.5 us (24%)
  waiting for transfers between devices  47.8 us (20%)
  matrix products  31.2 us (13%)
  other arithmetic  23.1 us (10%)
  starting transfers between devices  20.9 us (9%)
    all_to_all x1, blocking collectives, shards(): returned = lax.all_to_all(gridded, 'lat', 0, 0, tiled=True)  36 us
    all_to_all x1, waiting for transfers between devices, shards(): received = lax.all_to_all(coeffs, 'lat', 0, 0, tiled=True)  28.3 us
    all_to_all x1, blocking collectives, shards(): gridded = lax.all_to_all(gridded, 'mem', 0, 0, tiled=True)  21.9 us
    dot_general x1, matrix products, shards(): lax.dot_general(returned, table, (((0,), (1,)), ((), ())), preferred_elem...  18.6 us
    all_to_all x1, waiting for transfers between devices, shards(): parts = lax.all_to_all(parts, 'mem', 0, 0, tiled=True)  13.3 us
    reshape x2, local copies, waits for them, and re-layouts, shards(): gridded.reshape(mem_count, group, 2, channels, lat_count, band_rows)  11.7 us
    dot_general x1, matrix products, shards(): lax.dot_general(table, flattened, (((0,), (1,)), ((), ())), preferred_ele...  10.8 us
    convert_element_type x1, other arithmetic, fourier_table(): table = table.reshape(lon_count, -1).astype(jnp.bfloat16)  10.4 us
  transfers between devices with their start and end apart: 3, of which 3 were waited for; matrix products, arithmetic and copies ran while one was open for 14% of the time, Pallas kernels for 0%

profile of v1, /device:TPU:32, one launch (start us, length us, event | category | flops | bytes accessed | tf_op | source)
XLA Modules:
  0.0 238.7 jit_solution(12540071874744602399)
XLA Ops:
  1.3 3.2 %gather_fusion = s32[768]{0:T(1024)S(1)} fusion(s32[704]{0:T(1024)S(1)} %copy-done.2, s32[1024]{0:T(1024)S(1)} %pad_clamp_fusion.1), kind=kCustom, calls=%fused_computation | custom fusion | bytes 9216 | tf_op jit(solution)/shard_map/jit(_take)/gather | solution.py:72
  5.5 0.6 compare_select_fusion.2
  6.1 4.7 %select_select_fusion.1 = (f32[64,1536]{1,0:T(8,128)S(1)}, f32[64,1536]{1,0:T(8,128)}, f32[64,1536]{1,0:T(8,128)}, f32[64,1536]{1,0:T(8,128)}) fusion(s32[1536]{0:T(1024)S(1)} %mul.263, s32[64]{0:T(128)} %iota_multiply_fusion.2, pred[1536]{0:T(1024)(128)(4,1)} %fusion.29, pred[1536]{0:T(1024)(128)(4,1)S(1)} %broadcast_in_dim.68), kind=kLoop, calls=%fused_computation.43 | loop fusion | flops 3342336 | bytes 1582336 | tf_op jit(solution)/shard_map/jit(_where)/select_n | solution.py:23
  10.7 10.4 %add_convert_fusion = bf16[64,64,1536]{2,1,0:T(8,128)(2,1)} fusion(f32[64,1536]{1,0:T(8,128)} %get-tuple-element.16, f32[64,1536]{1,0:T(8,128)} %get-tuple-element.13, f32[64,1536]{1,0:T(8,128)} %get-tuple-element.17, f32[64,1536]{1,0:T(8,128)S(1)} %get-tuple-element.12), kind=kLoop, calls=%fused_computation.2 | loop fusion | flops 25165824 | bytes 14155776 | tf_op jit(solution)/shard_map/convert_element_type | solution.py:26
  21.1 10.8 %fusion = bf16[1536,384]{1,0:T(8,128)(2,1)} fusion(bf16[4096,1536]{1,0:T(8,128)(2,1)} %bitcast.45, bf16[384,4096]{1,0:T(8,128)(2,1)S(1)} %bitcast.43, f32[1536]{0:T(1024)S(1)} %copy-done.5), kind=kOutput, calls=%fused_computation.7 | convolution fusion | flops 4833017856 | bytes 16914432 | tf_op jit(solution)/shard_map/dot_general | solution.py:78
  31.9 9.7 %all-to-all-start.1 = ((bf16[32,48,384]{2,1,0:T(8,128)(2,1)}), bf16[32,48,384]{2,1,0:T(8,128)(2,1)S(1)}, u32[]{:S(2)}, u32[]{:S(2)}) async-start(bf16[32,48,384]{2,1,0:T(8,128)(2,1)} %bitcast.51), calls=%async_computation.1 | async-start | bytes 2359296 | tf_op jit(solution)/shard_map/all_to_all | solution.py:83
  41.6 3.5 %pad.4 = bf16[24,2,352,64]{2,3,1,0:T(8,128)(2,1)} pad(bf16[22,2,352,64]{2,3,1,0:T(8,128)(2,1)} %param.7, bf16[]{:T(256)} %constant.51.clone.1), padding=0_2x0_0x0_0x0_0 | pad | bytes 4145154 | tf_op jit(solution)/shard_map/jit(_pad)/pad | solution.py:64
  45.1 28.3 %all-to-all-done.1 = bf16[32,48,384]{2,1,0:T(8,128)(2,1)S(1)} async-done(((bf16[32,48,384]{2,1,0:T(8,128)(2,1)}), bf16[32,48,384]{2,1,0:T(8,128)(2,1)S(1)}, u32[]{:S(2)}, u32[]{:S(2)}) %all-to-all-start.1) | async-done | bytes 1179680 | tf_op jit(solution)/shard_map/all_to_all | solution.py:83
  73.4 6.6 %all-to-all-start = ((bf16[8,3,2,352,64]{3,4,2,1,0:T(8,128)(2,1)}), bf16[8,3,2,352,64]{3,4,2,1,0:T(8,128)(2,1)}, u32[]{:S(2)}, u32[]{:S(2)}) async-start(bf16[8,3,2,352,64]{3,4,2,1,0:T(8,128)(2,1)} %bitcast), calls=%async_computation | async-start | bytes 4718592 | tf_op jit(solution)/shard_map/all_to_all | solution.py:66
  80.1 1.3 fusion.8
  81.4 3.6 %stack.22 = bf16[1,16,8,3,2,12,32]{6,5,4,3,2,1,0:T(8,128)(2,1)S(1)} reshape(bf16[16,48,384]{2,1,0:T(8,128)(2,1)} %get-tuple-element.10) | data formatting | bytes 1179648 | tf_op jit(solution)/shard_map/stack | solution.py:88
  85.0 4.7 %stack.23 = bf16[1,16,8,3,2,12,32]{6,5,4,3,2,1,0:T(8,128)(2,1)} reshape(bf16[16,48,384]{2,1,0:T(8,128)(2,1)} %get-tuple-element.11) | data formatting | bytes 1179648 | tf_op jit(solution)/shard_map/stack | solution.py:88
  89.7 3.5 %maximum_bitcast_fusion = bf16[8,3,2,2,12,16,32]{6,4,3,1,0,5,2:T(8,128)(2,1)S(1)} fusion(bf16[1,16,8,3,2,12,32]{6,5,4,3,2,1,0:T(8,128)(2,1)} %stack.23, bf16[1,16,8,3,2,12,32]{6,5,4,3,2,1,0:T(8,128)(2,1)S(1)} %stack.22), kind=kLoop, calls=%fused_computation.3 | loop fusion | flops 589824 | bytes 2359296 | tf_op jit(solution)/shard_map/transpose | solution.py:90
  93.2 7.5 %copy.21 = bf16[8,3,2,2,12,16,32]{6,5,4,3,2,1,0:T(8,128)(2,1)} copy(bf16[8,3,2,2,12,16,32]{6,4,3,1,0,5,2:T(8,128)(2,1)S(1)} %maximum_bitcast_fusion) | data formatting | bytes 2359296 | tf_op jit(solution)/shard_map/transpose | solution.py:90
  100.8 7.3 %reshape.464 = bf16[8,144,512]{2,1,0:T(8,128)(2,1)} reshape(bf16[8,3,2,2,12,16,32]{6,5,4,3,2,1,0:T(8,128)(2,1)} %copy.21) | data formatting | bytes 2359296 | tf_op jit(solution)/shard_map/reshape | solution.py:90
  108.1 6.2 %all-to-all-done = bf16[8,3,2,352,64]{3,4,2,1,0:T(8,128)(2,1)} async-done(((bf16[8,3,2,352,64]{3,4,2,1,0:T(8,128)(2,1)}), bf16[8,3,2,352,64]{3,4,2,1,0:T(8,128)(2,1)}, u32[]{:S(2)}, u32[]{:S(2)}) %all-to-all-start) | async-done | bytes 2162720 | tf_op jit(solution)/shard_map/all_to_all | solution.py:66
  114.3 4.5 %all-to-all-start.2 = ((bf16[8,144,512]{2,1,0:T(8,128)(2,1)}), bf16[8,144,512]{2,1,0:T(8,128)(2,1)}, u32[]{:S(2)}, u32[]{:S(2)}) async-start(bf16[8,144,512]{2,1,0:T(8,128)(2,1)} %reshape.464), calls=%async_computation.2 | async-start | bytes 2359296 | tf_op jit(solution)/shard_map/all_to_all | solution.py:93
  118.8 0.6 gather_fusion.1
  119.7 1.9 copy.20
  121.6 13.3 %all-to-all-done.2 = bf16[8,144,512]{2,1,0:T(8,128)(2,1)} async-done(((bf16[8,144,512]{2,1,0:T(8,128)(2,1)}), bf16[8,144,512]{2,1,0:T(8,128)(2,1)}, u32[]{:S(2)}, u32[]{:S(2)}) %all-to-all-start.2) | async-done | bytes 1179680 | tf_op jit(solution)/shard_map/all_to_all | solution.py:93
  134.9 1.9 copy.22
  136.8 0.8 fusion.34
  138.2 1.1 copy-done.4
  139.3 1.0 fusion.3
  141.0 1.2 copy.28
  142.2 0.9 convert_element_type.71
  143.1 21.9 %all_to_all.25 = bf16[8,72,1024]{2,1,0:T(8,128)(2,1)S(1)} all-to-all(bf16[8,72,1024]{2,1,0:T(8,128)(2,1)S(1)} %convert_element_type.71), channel_id=1, replica_groups=mesh['mem'=8,'lat'=32] {'mem'}, dimensions={0} | all-to-all | bytes 2359296 | tf_op jit(solution)/shard_map/all_to_all | solution.py:115
  165.0 4.7 %reshape.467 = bf16[8,3,2,12,32,32]{5,4,3,2,1,0:T(8,128)(2,1)} reshape(bf16[8,72,1024]{2,1,0:T(8,128)(2,1)S(1)} %all_to_all.25) | data formatting | bytes 2359296 | tf_op jit(solution)/shard_map/reshape | solution.py:116
  169.8 7.0 %copy.45 = bf16[8,3,2,12,32,32]{5,3,2,1,0,4:T(8,128)(2,1)} copy(bf16[8,3,2,12,32,32]{5,4,3,2,1,0:T(8,128)(2,1)} %reshape.467) | data formatting | bytes 2359296 | tf_op jit(solution)/shard_map/reshape | solution.py:116
  176.7 7.4 %reshape.468 = bf16[32,48,384]{2,1,0:T(8,128)(2,1)S(1)} reshape(bf16[32,8,3,2,12,32]{5,4,3,2,1,0:T(8,128)(2,1)} %bitcast.44) | data formatting | bytes 2359296 | tf_op jit(solution)/shard_map/reshape | solution.py:117
  184.1 36.0 %all_to_all.26 = bf16[32,48,384]{2,1,0:T(8,128)(2,1)S(1)} all-to-all(bf16[32,48,384]{2,1,0:T(8,128)(2,1)S(1)} %reshape.468), channel_id=1, replica_groups=mesh['mem'=8,'lat'=32] {'lat'}, dimensions={0} | all-to-all | bytes 2359296 | tf_op jit(solution)/shard_map/all_to_all | solution.py:118
  220.1 18.6 %multiply_convert_fusion = bf16[384,4096]{1,0:T(8,128)(2,1)} fusion(bf16[1536,384]{1,0:T(8,128)(2,1)S(1)} %bitcast.52, bf16[4096,1536]{1,0:T(8,128)(2,1)} %bitcast.46), kind=kOutput, calls=%fused_computation.5 | convolution fusion | flops 4834983936 | bytes 16908288 | tf_op jit(solution)/shard_map/dot_general | solution.py:121
  (41 shorter events, 3.6 us)
Async XLA Ops:
  0.0 21.1 %copy-start = (bf16[1,3,4,32,4096]{4,3,2,1,0:T(8,128)(2,1)S(1)}, bf16[1,3,4,32,4096]{4,3,2,1,0:T(8,128)(2,1)}, u32[]{:S(2)}) copy-start(bf16[1,3,4,32,4096]{4,3,2,1,0:T(8,128)(2,1)} %param.6) | copy-start | bytes 9437188
  0.0 1.3 copy-start.2
  10.7 10.4 %copy-start.5 = (f32[1536]{0:T(1024)S(1)}, f32[1536]{0:T(1024)}, u32[]{:S(2)}) copy-start(f32[1536]{0:T(1024)} %compare_select_fusion.2) | copy-start | bytes 18436
  31.9 41.5 %all-to-all-start.1 = ((bf16[32,48,384]{2,1,0:T(8,128)(2,1)}), bf16[32,48,384]{2,1,0:T(8,128)(2,1)S(1)}, u32[]{:S(2)}, u32[]{:S(2)}) async-start(bf16[32,48,384]{2,1,0:T(8,128)(2,1)} %bitcast.51), calls=%async_computation.1 | async-start | bytes 2359296 | tf_op jit(solution)/shard_map/all_to_all | solution.py:83
  73.4 40.9 %all-to-all-start = ((bf16[8,3,2,352,64]{3,4,2,1,0:T(8,128)(2,1)}), bf16[8,3,2,352,64]{3,4,2,1,0:T(8,128)(2,1)}, u32[]{:S(2)}, u32[]{:S(2)}) async-start(bf16[8,3,2,352,64]{3,4,2,1,0:T(8,128)(2,1)} %bitcast), calls=%async_computation | async-start | bytes 4718592 | tf_op jit(solution)/shard_map/all_to_all | solution.py:66
  108.1 11.5 %copy-start.7 = (f32[4]{0:T(128)S(1)}, f32[4]{0:T(128)}, u32[]{:S(2)}) copy-start(f32[4]{0:T(128)} %param.9) | copy-start | bytes 52
  108.1 11.5 %copy-start.8 = (f32[4]{0:T(128)S(1)}, f32[4]{0:T(128)}, u32[]{:S(2)}) copy-start(f32[4]{0:T(128)} %param.10) | copy-start | bytes 52
  114.3 20.6 %all-to-all-start.2 = ((bf16[8,144,512]{2,1,0:T(8,128)(2,1)}), bf16[8,144,512]{2,1,0:T(8,128)(2,1)}, u32[]{:S(2)}, u32[]{:S(2)}) async-start(bf16[8,144,512]{2,1,0:T(8,128)(2,1)} %reshape.464), calls=%async_computation.2 | async-start | bytes 2359296 | tf_op jit(solution)/shard_map/all_to_all | solution.py:93
  121.6 16.0 %copy-start.3 = (bf16[3,2,352,8,64]{2,4,3,1,0:T(8,128)(2,1)}, bf16[3,2,352,8,64]{2,4,3,1,0:T(8,128)(2,1)S(1)}, u32[]{:S(2)}) copy-start(bf16[3,2,352,8,64]{2,4,3,1,0:T(8,128)(2,1)S(1)} %copy.20) | copy-start | bytes 6488068
  137.6 1.7 copy-start.4
  139.3 1.0 copy-start.6
  220.1 18.6 %copy-start.1 = (bf16[1,3,4,32,4096]{4,3,2,1,0:T(8,128)(2,1)S(1)}, bf16[1,3,4,32,4096]{4,3,2,1,0:T(8,128)(2,1)}, u32[]{:S(2)}) copy-start(bf16[1,3,4,32,4096]{4,3,2,1,0:T(8,128)(2,1)} %param.6) | copy-start | bytes 9437188
